TPU v7x, 256 devices: a whole 4x4x8 slice. The times are simulated.
256 devices in a mesh: seq: 32 (over x, z), head: 8 (over y, core).
Axes of the slice: x: 4, y: 4, z: 8, core: 2. Of those that a mesh axis runs over, the one named last changes fastest.
Arguments:
- att_query: bfloat16 [8192, 16, 128], P('seq', 'head'), may hold values from -9 to 9
- att_key: bfloat16 [8192, 16, 128], P('seq', 'head'), may hold values from -9 to 9
- att_value: bfloat16 [8192, 16, 128], P('seq', 'head'), may hold values from -6 to 6
- norm_gain: float32 [16, 128], P('head'), may hold values from 0.1 to 1.9
- dn_query: bfloat16 [8192, 16, 128], P('seq', 'head'), may hold values from -6 to 6
- dn_key: bfloat16 [8192, 16, 128], P('seq', 'head'), may hold values from -4 to 4
- write_rate: float32 [8192, 16], P('seq', 'head'), may hold values from 0.04 to 0.9
- log_decay: float32 [8192, 16], P('seq', 'head'), may hold values from -1 to 0
- out_grad: bfloat16 [8192, 16, 128], P('seq', 'head'), may hold values from -6 to 6
Outputs:
- block_out: bfloat16 [8192, 16, 128], P('seq', 'head')
- att_query_grad: bfloat16 [8192, 16, 128], P('seq', 'head')
- att_key_grad: bfloat16 [8192, 16, 128], P('seq', 'head')
- att_value_grad: bfloat16 [8192, 16, 128], P('seq', 'head')
- gain_grad: float32 [16, 128], P('head')
- dn_query_grad: bfloat16 [8192, 16, 128], P('seq', 'head')
- dn_key_grad: bfloat16 [8192, 16, 128], P('seq', 'head')
- rate_grad: float32 [8192, 16], P('seq', 'head')
- decay_grad: float32 [8192, 16], P('seq', 'head')
All inputs are finite; a program needn't handle non-finite values.
Results may differ from a plain program's by a relative error of at most 0.018.
Values may be sent and summed in bfloat16 or wider, within the bound.
No kernel may reach another device: no remote copies, remote signals or barrier semaphores. Data moves between devices by JAX's collectives and lax.ppermute only.
A program may use at most 64 MiB of HBM per device.

v0:
```python
import jax
import jax.numpy as jnp
from jax import lax
from jax.sharding import PartitionSpec as P

WIN = 1024
CH = 64
MATMUL_ACCURACY = lax.Precision.HIGHEST
EPSILON = 1e-06


def shifted_2(block, axis, distance):
    devices = range(lax.axis_size(axis))
    route = [(i - distance, i) for i in devices if i - distance in devices]
    return lax.ppermute(block, axis, route)


def unit_rows(matrix):
    return matrix * lax.rsqrt(jnp.sum(matrix * matrix, axis=-1, keepdims=True) + EPSILON)


def delta_block(memory_state, pieces):
    query_vectors, key_vectors, value_rows, rate_rows, decay_rows = pieces
    length = key_vectors.shape[1]
    lower = jnp.tril(jnp.ones((length, length), jnp.float32))
    strict = lower - jnp.eye(length, dtype=jnp.float32)
    running_state = jnp.cumsum(decay_rows, axis=1)
    ratio = jnp.exp((running_state[:, :, None] - running_state[:, None, :]) * lower) * lower
    state_increment = jnp.exp(running_state)
    intersection = jnp.einsum("htk,hsk->hts", key_vectors, key_vectors, precision=MATMUL_ACCURACY)
    system = (
        jnp.eye(length, dtype=jnp.float32) + rate_rows[:, :, None] * ratio * strict * intersection
    )
    retrieved_values = jnp.einsum(
        "nex,nxp->nep", key_vectors, memory_state, precision=MATMUL_ACCURACY
    )
    target = rate_rows[:, :, None] * (value_rows - state_increment[:, :, None] * retrieved_values)
    newest_state = jax.scipy.linalg.solve_triangular(system, target, lower=True, unit_diagonal=True)
    local_scores = (
        jnp.einsum("htk,hsk->hts", query_vectors, key_vectors, precision=MATMUL_ACCURACY) * ratio
    )
    state_output = state_increment[:, :, None] * jnp.einsum(
        "nex,nxp->nep", query_vectors, memory_state, precision=MATMUL_ACCURACY
    )
    state_output = state_output + jnp.einsum(
        "hts,hsv->htv", local_scores, newest_state, precision=MATMUL_ACCURACY
    )
    retained_state = jnp.exp(running_state[:, -1:] - running_state)
    memory_state = jnp.exp(running_state[:, -1])[:, None, None] * memory_state + jnp.einsum(
        "wpa,wpn->wan",
        key_vectors * retained_state[:, :, None],
        newest_state,
        precision=MATMUL_ACCURACY,
    )
    return (memory_state, state_output)


def delta_sweep(memory_state, query_vectors, key_vectors, value_rows, rate_rows, decay_rows):
    head_count, length = (key_vectors.shape[0], key_vectors.shape[1])
    blocks = length // CH

    def cut_blocks(array):
        return jnp.moveaxis(array.reshape((head_count, blocks, CH) + array.shape[2:]), 1, 0)

    last_state, state_output = lax.scan(
        delta_block,
        memory_state,
        (
            cut_blocks(query_vectors),
            cut_blocks(key_vectors),
            cut_blocks(value_rows),
            cut_blocks(rate_rows),
            cut_blocks(decay_rows),
        ),
    )
    return (
        last_state,
        jnp.moveaxis(state_output, 0, 1).reshape(head_count, length, state_output.shape[-1]),
    )


def window_softmax(rows_here, keys_here, values_here, alive_keys):
    block_rows = rows_here.shape[0]
    span_rows = keys_here.shape[0]
    reach_back = span_rows - block_rows
    scores = jnp.einsum("qhd,khd->hqk", rows_here, keys_here) * rows_here.shape[-1] ** (-0.5)
    query_pos = jnp.arange(block_rows, dtype=jnp.int32)[:, None]
    key_pos = jnp.arange(span_rows, dtype=jnp.int32)[None, :]
    allowed = (key_pos > query_pos) & (key_pos <= query_pos + reach_back) & alive_keys[None, :]
    scores = jnp.where(allowed[None], scores, -1e30)
    shifted = jnp.exp(scores - jnp.max(scores, axis=-1, keepdims=True))
    weights_bf = (shifted / jnp.sum(shifted, axis=-1, keepdims=True)).astype(jnp.bfloat16)
    return jnp.einsum("hqk,khd->qhd", weights_bf.astype(jnp.float32), values_here)


def attend(query_vectors, key_vectors, value_rows, alive_keys):
    outputs = [window_softmax(query_vectors, key_vectors, value_rows, alive_keys)]
    return jnp.concatenate(outputs, axis=0)


def apply_map(matrix, operand):
    return jnp.einsum("hij,hjv->hiv", matrix, operand, precision=MATMUL_ACCURACY)


def body(
    att_query, att_key, att_value, norm_gain, dn_query, dn_key, write_rate, log_decay, out_grad
):
    row_count, head_count, head_width = att_query.shape
    rim_rows = min(WIN, row_count)
    reach_back = max(1, WIN // row_count)
    my_shard = lax.axis_index("seq")
    shard_count = lax.axis_size("seq")
    older_keys = []
    older_values = []
    for offset in range(reach_back):
        came_key, came_value = shifted_2((att_key, att_value), "seq", offset + 1)
        older_keys.insert(0, came_key)
        older_values.insert(0, came_value)
    all_keys = jnp.concatenate(older_keys + [att_key], axis=0).astype(jnp.float32)
    all_values = jnp.concatenate(older_values + [att_value], axis=0).astype(jnp.float32)
    alive_keys = my_shard * row_count - WIN + jnp.arange(WIN + row_count, dtype=jnp.int32) >= 0

    def attention_core(query_vectors, key_vectors, value_rows):
        return attend(query_vectors, key_vectors, value_rows, alive_keys)

    attended, attention_pull = jax.vjp(
        attention_core, att_query.astype(jnp.float32), all_keys, all_values
    )
    square_part = jnp.sum(attended * attended, axis=(1, 2))
    square_all = lax.psum(square_part, "head")
    features = head_count * lax.axis_size("head") * head_width
    inverse = lax.rsqrt(square_all / features + EPSILON)
    scaled = attended * inverse[:, None, None]
    values = (scaled * norm_gain[None]).astype(jnp.bfloat16)
    query_heads = jnp.swapaxes(dn_query, 0, 1).astype(jnp.float32)
    key_heads = jnp.swapaxes(dn_key, 0, 1).astype(jnp.float32)
    value_heads = jnp.swapaxes(values, 0, 1)
    rate_heads = write_rate.T
    decay_heads = log_decay.T
    identity = jnp.broadcast_to(
        jnp.eye(head_width, dtype=jnp.float32), (head_count, head_width, head_width)
    )
    seed_state = jnp.concatenate(
        [identity, jnp.zeros((head_count, head_width, head_width), jnp.float32)], axis=-1
    )
    folded_values = jnp.concatenate(
        [jnp.zeros(value_heads.shape, jnp.float32), value_heads.astype(jnp.float32)], axis=-1
    )
    summary, unused_out = delta_sweep(
        seed_state,
        unit_rows(query_heads),
        unit_rows(key_heads),
        folded_values,
        rate_heads,
        decay_heads,
    )
    carry_map = summary[..., :head_width]
    carry_add = summary[..., head_width:]
    empty_state = jnp.zeros_like(carry_add)

    def relay(turn, current):
        return shifted_2(apply_map(carry_map, current) + carry_add, "seq", 1)

    start_state = lax.fori_loop(0, shard_count - 1, relay, empty_state)

    def local_delta(start_in, query_in, key_in, value_in, rate_in, decay_in):
        last_state, state_output = delta_sweep(
            start_in,
            unit_rows(query_in),
            unit_rows(key_in),
            value_in.astype(jnp.float32),
            rate_in,
            decay_in,
        )
        return (state_output, last_state)

    (state_output, last_state), delta_pull = jax.vjp(
        local_delta, start_state, query_heads, key_heads, value_heads, rate_heads, decay_heads
    )
    cotangent = jnp.swapaxes(out_grad, 0, 1).astype(jnp.float32)
    own_back = delta_pull((cotangent, empty_state))[0]
    flipped = jnp.swapaxes(carry_map, 1, 2)

    def relay_back(turn, current):
        return shifted_2(apply_map(flipped, current) + own_back, "seq", -1)

    later_grad = lax.fori_loop(0, shard_count - 1, relay_back, empty_state)
    delta_grads = delta_pull((cotangent, later_grad))
    value_grad = jnp.swapaxes(delta_grads[3], 0, 1).astype(jnp.float32)
    weighted = value_grad * norm_gain[None]
    dot_part = jnp.sum(weighted * attended, axis=(1, 2))
    gain_part = jnp.sum(value_grad * scaled, axis=0)
    dot_all = lax.psum(dot_part, "head")
    gain_grad = lax.psum(gain_part, "seq")
    attended_grad = (
        inverse[:, None, None] * weighted
        - attended * (inverse * inverse * inverse * dot_all / features)[:, None, None]
    )
    query_grad, keys_grad, values_grad = attention_pull(attended_grad)
    own_key_grad = keys_grad[WIN:]
    own_value_grad = values_grad[WIN:]
    extra_key = jnp.zeros((rim_rows, head_count, head_width), jnp.float32)
    extra_value = jnp.zeros((rim_rows, head_count, head_width), jnp.float32)
    for offset in range(reach_back):
        segment = reach_back - 1 - offset
        sent_key = keys_grad[segment * rim_rows : (segment + 1) * rim_rows]
        sent_value = values_grad[segment * rim_rows : (segment + 1) * rim_rows]
        came_key, came_value = (
            shifted_2(sent_key.astype(jnp.bfloat16), "seq", -(offset + 1)).astype(sent_key.dtype),
            shifted_2(sent_value.astype(jnp.bfloat16), "seq", -(offset + 1)).astype(
                sent_value.dtype
            ),
        )
        extra_key = extra_key + came_key
        extra_value = extra_value + came_value
    own_key_grad = own_key_grad.at[row_count - rim_rows :].add(extra_key)
    own_value_grad = own_value_grad.at[row_count - rim_rows :].add(extra_value)
    block_out = jnp.swapaxes(state_output, 0, 1).astype(jnp.bfloat16)
    return (
        block_out,
        query_grad.astype(jnp.bfloat16),
        own_key_grad.astype(jnp.bfloat16),
        own_value_grad.astype(jnp.bfloat16),
        gain_grad,
        jnp.swapaxes(delta_grads[1], 0, 1).astype(jnp.bfloat16),
        jnp.swapaxes(delta_grads[2], 0, 1).astype(jnp.bfloat16),
        delta_grads[4].T,
        delta_grads[5].T,
    )


def solution(mesh):
    return jax.shard_map(
        body,
        mesh=mesh,
        in_specs=(
            P("seq", "head", None),
            P("seq", "head", None),
            P("seq", "head", None),
            P("head", None),
            P("seq", "head", None),
            P("seq", "head", None),
            P("seq", "head"),
            P("seq", "head"),
            P("seq", "head", None),
        ),
        out_specs=(
            P("seq", "head", None),
            P("seq", "head", None),
            P("seq", "head", None),
            P("seq", "head", None),
            P("head", None),
            P("seq", "head", None),
            P("seq", "head", None),
            P("seq", "head"),
            P("seq", "head"),
        ),
        check_vma=False,
    )
```

profile of v0, /device:TPU:162, one launch (start us, length us, event | category | flops | bytes accessed | tf_op | source)
XLA Modules:
  0.0 1278.0 jit_solution(2413856035602274087)
XLA Ops:
  59.0 14.4 %psum.21 = f32[256]{0:T(256)S(1)} all-reduce(f32[256]{0:T(256)S(1)} %get-tuple-element.2481), channel_id=1, replica_groups=mesh['seq'=32,'head'=8] {'head'}, use_global_device_ids=true, to_apply=%region_4.5 | all-reduce | flops 256 | bytes 2048 | tf_op jit(solution)/shard_map/psum | solution.py:130
  78.7 69.7 %while.136 = (s32[]{:T(128)}, f32[2,128,256]{2,1,0:T(8,128)S(1)}, f32[4,2,64]{2,1,0:T(2,128)}, f32[4,2,64,128]{3,2,1,0:T(8,128)S(1)}, f32[4,2,64]{2,1,0:T(2,128)...) while((s32[]{:T(128)}, f32[2,128,256]{2,1,0:T(8,128)S(1)}, f32[4,2,64]{2,1,0:T(2,128)}, ...), condition=%wide.region_7.8_spmd, body=%wide.region_5.0_spmd.sunk | while | flops 138780736 | bytes 1925833 | solution.py:65
  82.6 11.2 custom-call.55
  100.0 11.2 custom-call.55
  117.4 11.2 custom-call.55
  134.9 11.2 custom-call.55
  152.2 311.7 %while.137 = (s32[]{:T(128)}, f32[2,128,128]{2,1,0:T(8,128)S(1)}, f32[2,128,128]{2,1,0:T(8,128)S(1)}, f32[2,128,128]{2,1,0:T(8,128)S(1)}, s32[]{:T(128)}) while((s32[]{:T(128)}, f32[2,128,128]{2,1,0:T(8,128)S(1)}, f32[2,128,128]{2,1,0:T(8,128)S(1)}, f32[2,128,128]{2,1,0:T(8,128)S(1)}, s32[]{:T(128)}) %tuple.298), condition=%wide.region_9.10_spmd, body=%wide.region_8.9_spmd.sunk | while | flops 50364416 | bytes 1048677 | solution.py:164
  467.6 105.8 %while.139 = (s32[]{:T(128)}, f32[2,128,128]{2,1,0:T(8,128)S(1)}, bf16[4,2,64,128]{3,2,1,0:T(8,128)(2,1)}, f32[4,2,64,64]{3,2,1,0:T(8,128)}, f32[4,2,64]{2,1,0:T...) while((s32[]{:T(128)}, f32[2,128,128]{2,1,0:T(8,128)S(1)}, ...), condition=%wide.region_13.14_spmd.clone.clone, body=%wide.region_11.13_spmd.clone.clone.sunk | while | flops 126304576 | bytes 3452789 | solution.py:65
  472.0 10.6 custom-call.56
  498.4 10.6 custom-call.56
  524.8 10.6 custom-call.56
  551.3 10.6 custom-call.56
  574.0 65.0 %while.141 = (s32[]{:T(128)}, f32[2,128,128]{2,1,0:T(8,128)S(1)}, f32[4,2,1,1]{1,3,2,0:T(1,128)}, f32[4,2,64,128]{3,2,1,0:T(8,128)}, f32[4,2,64,1]{2,1,3,0:T(2,1...) while((s32[]{:T(128)}, f32[2,128,128]{2,1,0:T(8,128)S(1)}, ...), condition=%wide.region_15.17_spmd.clone, body=%wide.region_14.16_spmd.clone.sunk | while | flops 100937792 | bytes 1587911 | solution.py:65
  577.7 9.8 custom-call.59
  594.0 9.8 custom-call.59
  610.2 9.8 custom-call.59
  626.5 9.8 custom-call.59
  639.0 292.8 %while.138 = (s32[]{:T(128)}, f32[2,128,128]{2,1,0:T(8,128)S(1)}, f32[2,128,128]{2,1,0:T(8,128)S(1)}, f32[2,128,128]{2,1,0:T(8,128)S(1)}, s32[]{:T(128)}) while((s32[]{:T(128)}, f32[2,128,128]{2,1,0:T(8,128)S(1)}, f32[2,128,128]{2,1,0:T(8,128)S(1)}, f32[2,128,128]{2,1,0:T(8,128)S(1)}, s32[]{:T(128)}) %tuple.319), condition=%wide.region_17.19_spmd, body=%wide.region_16.18_spmd.sunk | while | flops 50364416 | bytes 1048677 | solution.py:187
  812.3 8.7 collective-permute-done.1
  935.1 192.5 %while.140 = (s32[]{:T(128)}, f32[2,128,128]{2,1,0:T(8,128)S(1)}, f32[4,2,64,128]{3,2,1,0:T(8,128)}, f32[4,2,64,128]{3,2,1,0:T(8,128)}, bf16[4,2,64,128]{3,2,0,1...) while((s32[]{:T(128)}, f32[2,128,128]{2,1,0:T(8,128)S(1)}, ...), condition=%wide.region_29.31_spmd.clone.clone, body=%wide.region_18.30_spmd.clone.clone.sunk | while | flops 258761408 | bytes 5408265 | solution.py:65
  939.3 9.8 custom-call.58
  953.5 9.8 custom-call.57
  987.4 9.8 custom-call.58
  1001.6 9.8 custom-call.57
  1035.5 9.8 custom-call.58
  1049.7 9.8 custom-call.57
  1083.6 9.8 custom-call.58
  1097.8 9.8 custom-call.57
  1130.5 12.4 psum.22
  1161.3 13.9 %collective-permute-start.16 = (bf16[256,2,128]{0,2,1:T(8,128)(2,1)S(1)}, bf16[256,2,128]{0,2,1:T(8,128)(2,1)S(1)}, u32[]{:S(2)}, u32[]{:S(2)}) collective-permute-start(bf16[256,2,128]{0,2,1:T(8,128)(2,1)S(1)} %get-tuple-element.2471), channel_id=1, source_target_pairs={{24,0},{32,8},{40,16},{48,24},{56,32},{64,40},{72,48},{80,56},{88,... | collective-permute-start | bytes 393224 | tf_op jit(solution)/shard_map/ppermute | solution.py:15
  1179.9 67.6 %psum.23 = f32[2,128]{1,0:T(2,128)} all-reduce(f32[2,128]{1,0:T(2,128)S(1)} %copy-done.42), channel_id=1, replica_groups=mesh['seq'=32,'head'=8] {'seq'}, use_global_device_ids=true, to_apply=%region_36.38 | all-reduce | flops 256 | bytes 2048 | tf_op jit(solution)/shard_map/psum | solution.py:194
  1253.7 10.1 collective-permute-start.12
  (769 shorter events, 941.7 us)
Async XLA Ops:
  1.7 32.5 %collective-permute-start.6 = (bf16[256,2,128]{2,0,1:T(8,128)(2,1)S(1)}, bf16[256,2,128]{2,0,1:T(8,128)(2,1)S(1)}, u32[]{:S(2)}, u32[]{:S(2)}) collective-permute-start(bf16[256,2,128]{2,0,1:T(8,128)(2,1)S(1)} %copy.247), channel_id=1, source_target_pairs={{0,32},{8,40},{16,48},{24,56},{32,64},{40,72},{48,80},{56,88},{64,... | collective-permute-start | bytes 393224 | tf_op jit(solution)/shard_map/ppermute | solution.py:15
  4.2 36.0 %collective-permute-start.7 = (bf16[256,2,128]{2,0,1:T(8,128)(2,1)S(1)}, bf16[256,2,128]{2,0,1:T(8,128)(2,1)S(1)}, u32[]{:S(2)}, u32[]{:S(2)}) collective-permute-start(bf16[256,2,128]{2,0,1:T(8,128)(2,1)S(1)} %copy.247), channel_id=1, source_target_pairs={{0,24},{8,32},{16,40},{24,48},{32,56},{40,64},{48,72},{56,80},{64,... | collective-permute-start | bytes 393224 | tf_op jit(solution)/shard_map/ppermute | solution.py:15
  11.9 30.7 %collective-permute-start.8 = (bf16[256,2,128]{2,0,1:T(8,128)(2,1)S(1)}, bf16[256,2,128]{2,0,1:T(8,128)(2,1)S(1)}, u32[]{:S(2)}, u32[]{:S(2)}) collective-permute-start(bf16[256,2,128]{2,0,1:T(8,128)(2,1)S(1)} %copy.247), channel_id=1, source_target_pairs={{0,16},{8,24},{16,32},{24,40},{32,48},{40,56},{48,64},{56,72},{64,... | collective-permute-start | bytes 393224 | tf_op jit(solution)/shard_map/ppermute | solution.py:15
  15.3 29.8 %collective-permute-start.9 = (bf16[256,2,128]{2,0,1:T(8,128)(2,1)S(1)}, bf16[256,2,128]{2,0,1:T(8,128)(2,1)S(1)}, u32[]{:S(2)}, u32[]{:S(2)}) collective-permute-start(bf16[256,2,128]{2,0,1:T(8,128)(2,1)S(1)} %copy.247), channel_id=1, source_target_pairs={{0,8},{8,16},{16,24},{24,32},{32,40},{40,48},{48,56},{56,64},{64,7... | collective-permute-start | bytes 393224 | tf_op jit(solution)/shard_map/ppermute | solution.py:15
  30.2 17.6 %collective-permute-start.2 = (bf16[256,2,128]{0,2,1:T(8,128)(2,1)S(1)}, bf16[256,2,128]{0,2,1:T(8,128)(2,1)S(1)}, u32[]{:S(2)}, u32[]{:S(2)}) collective-permute-start(bf16[256,2,128]{0,2,1:T(8,128)(2,1)S(1)} %copy.242), channel_id=1, source_target_pairs={{0,32},{8,40},{16,48},{24,56},{32,64},{40,72},{48,80},{56,88},{64,... | collective-permute-start | bytes 393224 | tf_op jit(solution)/shard_map/ppermute | solution.py:15
  34.2 15.9 %collective-permute-start.3 = (bf16[256,2,128]{0,2,1:T(8,128)(2,1)S(1)}, bf16[256,2,128]{0,2,1:T(8,128)(2,1)S(1)}, u32[]{:S(2)}, u32[]{:S(2)}) collective-permute-start(bf16[256,2,128]{0,2,1:T(8,128)(2,1)S(1)} %copy.242), channel_id=1, source_target_pairs={{0,24},{8,32},{16,40},{24,48},{32,56},{40,64},{48,72},{56,80},{64,... | collective-permute-start | bytes 393224 | tf_op jit(solution)/shard_map/ppermute | solution.py:15
  40.2 16.7 %collective-permute-start.4 = (bf16[256,2,128]{0,2,1:T(8,128)(2,1)S(1)}, bf16[256,2,128]{0,2,1:T(8,128)(2,1)S(1)}, u32[]{:S(2)}, u32[]{:S(2)}) collective-permute-start(bf16[256,2,128]{0,2,1:T(8,128)(2,1)S(1)} %copy.242), channel_id=1, source_target_pairs={{0,16},{8,24},{16,32},{24,40},{32,48},{40,56},{48,64},{56,72},{64,... | collective-permute-start | bytes 393224 | tf_op jit(solution)/shard_map/ppermute | solution.py:15
  42.6 15.2 %collective-permute-start.5 = (bf16[256,2,128]{0,2,1:T(8,128)(2,1)S(1)}, bf16[256,2,128]{0,2,1:T(8,128)(2,1)S(1)}, u32[]{:S(2)}, u32[]{:S(2)}) collective-permute-start(bf16[256,2,128]{0,2,1:T(8,128)(2,1)S(1)} %copy.242), channel_id=1, source_target_pairs={{0,8},{8,16},{16,24},{24,32},{32,40},{40,48},{48,56},{56,64},{64,7... | collective-permute-start | bytes 393224 | tf_op jit(solution)/shard_map/ppermute | solution.py:15
  198.9 9.5 collective-permute-start
  238.9 9.2 collective-permute-start
  279.3 9.9 collective-permute-start
  290.1 10.5 collective-permute-start
  362.2 9.6 collective-permute-start
  372.8 10.6 collective-permute-start
  639.2 9.3 collective-permute-start.1
  648.8 9.3 collective-permute-start.1
  658.4 9.4 collective-permute-start.1
  668.0 10.5 collective-permute-start.1
  678.8 10.1 collective-permute-start.1
  734.5 9.6 collective-permute-start.1
  744.3 10.3 collective-permute-start.1
  754.9 9.3 collective-permute-start.1
  810.4 10.6 collective-permute-start.1
  821.2 9.7 collective-permute-start.1
  1157.4 93.6 %collective-permute-start.14 = (bf16[256,2,128]{0,2,1:T(8,128)(2,1)S(1)}, bf16[256,2,128]{0,2,1:T(8,128)(2,1)S(1)}, u32[]{:S(2)}, u32[]{:S(2)}) collective-permute-start(bf16[256,2,128]{0,2,1:T(8,128)(2,1)S(1)} %get-tuple-element.2469), channel_id=1, source_target_pairs={{8,0},{16,8},{24,16},{32,24},{40,32},{48,40},{56,48},{64,56},{72,6... | collective-permute-start | bytes 393224 | tf_op jit(solution)/shard_map/ppermute | solution.py:15
  1159.4 94.3 %collective-permute-start.15 = (bf16[256,2,128]{0,2,1:T(8,128)(2,1)S(1)}, bf16[256,2,128]{0,2,1:T(8,128)(2,1)S(1)}, u32[]{:S(2)}, u32[]{:S(2)}) collective-permute-start(bf16[256,2,128]{0,2,1:T(8,128)(2,1)S(1)} %get-tuple-element.2472), channel_id=1, source_target_pairs={{16,0},{24,8},{32,16},{40,24},{48,32},{56,40},{64,48},{72,56},{80,... | collective-permute-start | bytes 393224 | tf_op jit(solution)/shard_map/ppermute | solution.py:15
  1161.3 102.5 %collective-permute-start.16 = (bf16[256,2,128]{0,2,1:T(8,128)(2,1)S(1)}, bf16[256,2,128]{0,2,1:T(8,128)(2,1)S(1)}, u32[]{:S(2)}, u32[]{:S(2)}) collective-permute-start(bf16[256,2,128]{0,2,1:T(8,128)(2,1)S(1)} %get-tuple-element.2471), channel_id=1, source_target_pairs={{24,0},{32,8},{40,16},{48,24},{56,32},{64,40},{72,48},{80,56},{88,... | collective-permute-start | bytes 393224 | tf_op jit(solution)/shard_map/ppermute | solution.py:15
  1175.2 90.5 %collective-permute-start.17 = (bf16[256,2,128]{0,2,1:T(8,128)(2,1)S(1)}, bf16[256,2,128]{0,2,1:T(8,128)(2,1)S(1)}, u32[]{:S(2)}, u32[]{:S(2)}) collective-permute-start(bf16[256,2,128]{0,2,1:T(8,128)(2,1)S(1)} %get-tuple-element.2470), channel_id=1, source_target_pairs={{32,0},{40,8},{48,16},{56,24},{64,32},{72,40},{80,48},{88,56},{96,... | collective-permute-start | bytes 393224 | tf_op jit(solution)/shard_map/ppermute | solution.py:15
  1177.2 90.4 %collective-permute-start.10 = (bf16[256,2,128]{2,0,1:T(8,128)(2,1)S(1)}, bf16[256,2,128]{2,0,1:T(8,128)(2,1)S(1)}, u32[]{:S(2)}, u32[]{:S(2)}) collective-permute-start(bf16[256,2,128]{2,0,1:T(8,128)(2,1)S(1)} %get-tuple-element.2473), channel_id=1, source_target_pairs={{8,0},{16,8},{24,16},{32,24},{40,32},{48,40},{56,48},{64,56},{72,6... | collective-permute-start | bytes 393224 | tf_op jit(solution)/shard_map/ppermute | solution.py:15
  1251.0 16.5 %collective-permute-start.11 = (bf16[256,2,128]{2,0,1:T(8,128)(2,1)S(1)}, bf16[256,2,128]{2,0,1:T(8,128)(2,1)S(1)}, u32[]{:S(2)}, u32[]{:S(2)}) collective-permute-start(bf16[256,2,128]{2,0,1:T(8,128)(2,1)S(1)} %get-tuple-element.2476), channel_id=1, source_target_pairs={{16,0},{24,8},{32,16},{40,24},{48,32},{56,40},{64,48},{72,56},{80,... | collective-permute-start | bytes 393224 | tf_op jit(solution)/shard_map/ppermute | solution.py:15
  1253.7 13.9 %collective-permute-start.12 = (bf16[256,2,128]{2,0,1:T(8,128)(2,1)S(1)}, bf16[256,2,128]{2,0,1:T(8,128)(2,1)S(1)}, u32[]{:S(2)}, u32[]{:S(2)}) collective-permute-start(bf16[256,2,128]{2,0,1:T(8,128)(2,1)S(1)} %get-tuple-element.2475), channel_id=1, source_target_pairs={{24,0},{32,8},{40,16},{48,24},{56,32},{64,40},{72,48},{80,56},{88,... | collective-permute-start | bytes 393224 | tf_op jit(solution)/shard_map/ppermute | solution.py:15
  1263.8 12.4 collective-permute-start.13
  (94 other events, 1288.2 us)
where the time goes:
time: 1290 us; the launch traced here: 1280 us
  waiting for transfers between devices  349 us (27%)
  starting transfers between devices  304 us (24%)
  other arithmetic  272 us (21%)
  matrix products  187 us (14%)
  blocking collectives  94.4 us (7%)
  local copies, waits for them, and re-layouts  67.5 us (5%)
    ppermute x78, waiting for transfers between devices, shifted_2(): return lax.ppermute(block, axis, route)  349 us
    ppermute x78, starting transfers between devices, shifted_2(): return lax.ppermute(block, axis, route)  304 us
    another operation x72, other arithmetic, delta_block(): jax.scipy.linalg.solve_triangular(system, target, lower=True, unit_diagon...  217 us
    psum x1, blocking collectives, body(): gain_grad = lax.psum(gain_part, 'seq')  67.6 us
    dot_general x62, matrix products, apply_map(): jnp.einsum('hij,hjv->hiv', matrix, operand, precision=MATMUL_ACCURACY)  37 us
  transfers between devices with their start and end apart: 78, of which 66 were waited for; matrix products, arithmetic and copies ran while one was open for 2% of the time, Pallas kernels for 0%

commit v1 on v0

--- a/solution.py
+++ b/solution.py
@@ -191,7 +191,11 @@
     dot_part = jnp.sum(weighted * attended, axis=(1, 2))
     gain_part = jnp.sum(value_grad * scaled, axis=0)
     dot_all = lax.psum(dot_part, "head")
-    gain_grad = lax.psum(gain_part, "seq")
+    gain_grad = gain_part
+    for hop in (1, 2, 4, 8, 16):
+        gain_grad = gain_grad + lax.ppermute(
+            gain_grad, "seq", [(dev, dev ^ hop) for dev in range(32)]
+        )
     attended_grad = (
         inverse[:, None, None] * weighted
         - attended * (inverse * inverse * inverse * dot_all / features)[:, None, None]

time: 1290 us -> 1240 us (0.961)
  blocking collectives: 94.4 us -> 26.8 us
  waiting for transfers between devices: 349 us -> 365 us
    psum x1 -> x0, blocking collectives: 67.6 us -> none  [body(): gain_grad = lax.psum(gain_part, 'seq')]
  transfers between devices with their start and end apart: 78 -> 83, of which waited for: 66 -> 71; matrix products, arithmetic and copies ran while one was open for 2% -> 2% of each run, Pallas kernels for 0% -> 0%
where the time goes in v1:
time: 1240 us; the launch traced here: 1230 us
  waiting for transfers between devices  365 us (29%)
  starting transfers between devices  307 us (25%)
  other arithmetic  273 us (22%)
  matrix products  187 us (15%)
  local copies, waits for them, and re-layouts  67.7 us (5%)
  blocking collectives  26.8 us (2%)
    ppermute x78, waiting for transfers between devices, shifted_2(): return lax.ppermute(block, axis, route)  353 us
    ppermute x78, starting transfers between devices, shifted_2(): return lax.ppermute(block, axis, route)  298 us
    another operation x72, other arithmetic, delta_block(): jax.scipy.linalg.solve_triangular(system, target, lower=True, unit_diagon...  217 us
    dot_general x62, matrix products, apply_map(): jnp.einsum('hij,hjv->hiv', matrix, operand, precision=MATMUL_ACCURACY)  37 us
  transfers between devices with their start and end apart: 83, of which 71 were waited for; matrix products, arithmetic and copies ran while one was open for 2% of the time, Pallas kernels for 0%

profile of v1, /device:TPU:162, one launch (start us, length us, event | category | flops | bytes accessed | tf_op | source)
XLA Modules:
  0.0 1230.4 jit_solution(16741582018237884326)
XLA Ops:
  59.0 14.4 %psum.14 = f32[256]{0:T(256)S(1)} all-reduce(f32[256]{0:T(256)S(1)} %get-tuple-element.2481), channel_id=1, replica_groups=mesh['seq'=32,'head'=8] {'head'}, use_global_device_ids=true, to_apply=%region_4.5 | all-reduce | flops 256 | bytes 2048 | tf_op jit(solution)/shard_map/psum | solution.py:130
  78.8 69.7 %while.136 = (s32[]{:T(128)}, f32[2,128,256]{2,1,0:T(8,128)S(1)}, f32[4,2,64]{2,1,0:T(2,128)}, f32[4,2,64,128]{3,2,1,0:T(8,128)S(1)}, f32[4,2,64]{2,1,0:T(2,128)...) while((s32[]{:T(128)}, f32[2,128,256]{2,1,0:T(8,128)S(1)}, f32[4,2,64]{2,1,0:T(2,128)}, ...), condition=%wide.region_7.8_spmd, body=%wide.region_5.0_spmd.sunk | while | flops 138780736 | bytes 1925833 | solution.py:65
  82.6 11.2 custom-call.55
  100.0 11.2 custom-call.55
  117.5 11.2 custom-call.55
  134.9 11.2 custom-call.55
  152.3 311.7 %while.137 = (s32[]{:T(128)}, f32[2,128,128]{2,1,0:T(8,128)S(1)}, f32[2,128,128]{2,1,0:T(8,128)S(1)}, f32[2,128,128]{2,1,0:T(8,128)S(1)}, s32[]{:T(128)}) while((s32[]{:T(128)}, f32[2,128,128]{2,1,0:T(8,128)S(1)}, f32[2,128,128]{2,1,0:T(8,128)S(1)}, f32[2,128,128]{2,1,0:T(8,128)S(1)}, s32[]{:T(128)}) %tuple.298), condition=%wide.region_9.10_spmd, body=%wide.region_8.9_spmd.sunk | while | flops 50364416 | bytes 1048677 | solution.py:164
  467.6 105.9 %while.139 = (s32[]{:T(128)}, f32[2,128,128]{2,1,0:T(8,128)S(1)}, bf16[4,2,64,128]{3,2,1,0:T(8,128)(2,1)}, f32[4,2,64,64]{3,2,1,0:T(8,128)}, f32[4,2,64]{2,1,0:T...) while((s32[]{:T(128)}, f32[2,128,128]{2,1,0:T(8,128)S(1)}, ...), condition=%wide.region_13.14_spmd.clone.clone, body=%wide.region_11.13_spmd.clone.clone.sunk | while | flops 126304576 | bytes 3452789 | solution.py:65
  472.0 10.6 custom-call.56
  498.5 10.6 custom-call.56
  525.0 10.6 custom-call.56
  551.4 10.6 custom-call.56
  574.1 65.0 %while.141 = (s32[]{:T(128)}, f32[2,128,128]{2,1,0:T(8,128)S(1)}, f32[4,2,1,1]{1,3,2,0:T(1,128)}, f32[4,2,64,128]{3,2,1,0:T(8,128)}, f32[4,2,64,1]{2,1,3,0:T(2,1...) while((s32[]{:T(128)}, f32[2,128,128]{2,1,0:T(8,128)S(1)}, ...), condition=%wide.region_15.17_spmd.clone, body=%wide.region_14.16_spmd.clone.sunk | while | flops 100937792 | bytes 1587911 | solution.py:65
  577.9 9.8 custom-call.59
  594.1 9.8 custom-call.59
  610.4 9.8 custom-call.59
  626.6 9.8 custom-call.59
  639.1 292.9 %while.138 = (s32[]{:T(128)}, f32[2,128,128]{2,1,0:T(8,128)S(1)}, f32[2,128,128]{2,1,0:T(8,128)S(1)}, f32[2,128,128]{2,1,0:T(8,128)S(1)}, s32[]{:T(128)}) while((s32[]{:T(128)}, f32[2,128,128]{2,1,0:T(8,128)S(1)}, f32[2,128,128]{2,1,0:T(8,128)S(1)}, f32[2,128,128]{2,1,0:T(8,128)S(1)}, s32[]{:T(128)}) %tuple.319), condition=%wide.region_17.19_spmd, body=%wide.region_16.18_spmd.sunk | while | flops 50364416 | bytes 1048677 | solution.py:187
  670.2 8.6 collective-permute-done.1
  812.5 8.7 collective-permute-done.1
  935.3 192.8 %while.140 = (s32[]{:T(128)}, f32[2,128,128]{2,1,0:T(8,128)S(1)}, f32[4,2,64,128]{3,2,1,0:T(8,128)}, f32[4,2,64,128]{3,2,1,0:T(8,128)}, bf16[4,2,64,128]{3,2,0,1...) while((s32[]{:T(128)}, f32[2,128,128]{2,1,0:T(8,128)S(1)}, ...), condition=%wide.region_29.31_spmd.clone.clone, body=%wide.region_18.30_spmd.clone.clone.sunk | while | flops 258761408 | bytes 5408265 | solution.py:65
  939.5 9.8 custom-call.58
  953.8 9.8 custom-call.57
  987.6 9.8 custom-call.58
  1001.9 9.8 custom-call.57
  1035.8 9.8 custom-call.58
  1050.1 9.8 custom-call.57
  1083.9 9.8 custom-call.58
  1098.2 9.8 custom-call.57
  1131.0 12.4 %psum.15 = f32[256]{0:T(256)S(1)} all-reduce(f32[256]{0:T(256)S(1)} %get-tuple-element.2245), channel_id=1, replica_groups=mesh['seq'=32,'head'=8] {'head'}, use_global_device_ids=true, to_apply=%region_31.33 | all-reduce | flops 256 | bytes 2048 | tf_op jit(solution)/shard_map/psum | solution.py:193
  1182.9 9.1 collective-permute-start.16
  1216.2 12.4 %collective-permute-done.12 = bf16[256,2,128]{2,0,1:T(8,128)(2,1)S(1)} collective-permute-done((bf16[256,2,128]{2,0,1:T(8,128)(2,1)S(1)}, bf16[256,2,128]{2,0,1:T(8,128)(2,1)S(1)}, u32[]{:S(2)}, u32[]{:S(2)}) %collective-permute-start.12) | collective-permute-done | bytes 131104 | tf_op jit(solution)/shard_map/ppermute | solution.py:15
  (783 shorter events, 955.6 us)
Async XLA Ops:
  1.7 32.5 %collective-permute-start.6 = (bf16[256,2,128]{2,0,1:T(8,128)(2,1)S(1)}, bf16[256,2,128]{2,0,1:T(8,128)(2,1)S(1)}, u32[]{:S(2)}, u32[]{:S(2)}) collective-permute-start(bf16[256,2,128]{2,0,1:T(8,128)(2,1)S(1)} %copy.247), channel_id=1, source_target_pairs={{0,32},{8,40},{16,48},{24,56},{32,64},{40,72},{48,80},{56,88},{64,... | collective-permute-start | bytes 393224 | tf_op jit(solution)/shard_map/ppermute | solution.py:15
  4.2 36.0 %collective-permute-start.7 = (bf16[256,2,128]{2,0,1:T(8,128)(2,1)S(1)}, bf16[256,2,128]{2,0,1:T(8,128)(2,1)S(1)}, u32[]{:S(2)}, u32[]{:S(2)}) collective-permute-start(bf16[256,2,128]{2,0,1:T(8,128)(2,1)S(1)} %copy.247), channel_id=1, source_target_pairs={{0,24},{8,32},{16,40},{24,48},{32,56},{40,64},{48,72},{56,80},{64,... | collective-permute-start | bytes 393224 | tf_op jit(solution)/shard_map/ppermute | solution.py:15
  11.9 30.7 %collective-permute-start.8 = (bf16[256,2,128]{2,0,1:T(8,128)(2,1)S(1)}, bf16[256,2,128]{2,0,1:T(8,128)(2,1)S(1)}, u32[]{:S(2)}, u32[]{:S(2)}) collective-permute-start(bf16[256,2,128]{2,0,1:T(8,128)(2,1)S(1)} %copy.247), channel_id=1, source_target_pairs={{0,16},{8,24},{16,32},{24,40},{32,48},{40,56},{48,64},{56,72},{64,... | collective-permute-start | bytes 393224 | tf_op jit(solution)/shard_map/ppermute | solution.py:15
  15.3 29.8 %collective-permute-start.9 = (bf16[256,2,128]{2,0,1:T(8,128)(2,1)S(1)}, bf16[256,2,128]{2,0,1:T(8,128)(2,1)S(1)}, u32[]{:S(2)}, u32[]{:S(2)}) collective-permute-start(bf16[256,2,128]{2,0,1:T(8,128)(2,1)S(1)} %copy.247), channel_id=1, source_target_pairs={{0,8},{8,16},{16,24},{24,32},{32,40},{40,48},{48,56},{56,64},{64,7... | collective-permute-start | bytes 393224 | tf_op jit(solution)/shard_map/ppermute | solution.py:15
  30.2 17.6 %collective-permute-start.2 = (bf16[256,2,128]{0,2,1:T(8,128)(2,1)S(1)}, bf16[256,2,128]{0,2,1:T(8,128)(2,1)S(1)}, u32[]{:S(2)}, u32[]{:S(2)}) collective-permute-start(bf16[256,2,128]{0,2,1:T(8,128)(2,1)S(1)} %copy.242), channel_id=1, source_target_pairs={{0,32},{8,40},{16,48},{24,56},{32,64},{40,72},{48,80},{56,88},{64,... | collective-permute-start | bytes 393224 | tf_op jit(solution)/shard_map/ppermute | solution.py:15
  34.2 15.9 %collective-permute-start.3 = (bf16[256,2,128]{0,2,1:T(8,128)(2,1)S(1)}, bf16[256,2,128]{0,2,1:T(8,128)(2,1)S(1)}, u32[]{:S(2)}, u32[]{:S(2)}) collective-permute-start(bf16[256,2,128]{0,2,1:T(8,128)(2,1)S(1)} %copy.242), channel_id=1, source_target_pairs={{0,24},{8,32},{16,40},{24,48},{32,56},{40,64},{48,72},{56,80},{64,... | collective-permute-start | bytes 393224 | tf_op jit(solution)/shard_map/ppermute | solution.py:15
  40.2 16.7 %collective-permute-start.4 = (bf16[256,2,128]{0,2,1:T(8,128)(2,1)S(1)}, bf16[256,2,128]{0,2,1:T(8,128)(2,1)S(1)}, u32[]{:S(2)}, u32[]{:S(2)}) collective-permute-start(bf16[256,2,128]{0,2,1:T(8,128)(2,1)S(1)} %copy.242), channel_id=1, source_target_pairs={{0,16},{8,24},{16,32},{24,40},{32,48},{40,56},{48,64},{56,72},{64,... | collective-permute-start | bytes 393224 | tf_op jit(solution)/shard_map/ppermute | solution.py:15
  42.6 15.2 %collective-permute-start.5 = (bf16[256,2,128]{0,2,1:T(8,128)(2,1)S(1)}, bf16[256,2,128]{0,2,1:T(8,128)(2,1)S(1)}, u32[]{:S(2)}, u32[]{:S(2)}) collective-permute-start(bf16[256,2,128]{0,2,1:T(8,128)(2,1)S(1)} %copy.242), channel_id=1, source_target_pairs={{0,8},{8,16},{16,24},{24,32},{32,40},{40,48},{48,56},{56,64},{64,7... | collective-permute-start | bytes 393224 | tf_op jit(solution)/shard_map/ppermute | solution.py:15
  199.0 9.4 collective-permute-start
  279.3 10.0 collective-permute-start
  290.2 10.5 collective-permute-start
  362.3 9.6 collective-permute-start
  372.8 10.6 collective-permute-start
  639.4 9.3 collective-permute-start.1
  649.0 9.3 collective-permute-start.1
  658.6 9.4 collective-permute-start.1
  668.2 10.5 collective-permute-start.1
  679.0 10.0 collective-permute-start.1
  734.6 9.6 collective-permute-start.1
  744.5 10.3 collective-permute-start.1
  755.1 9.3 collective-permute-start.1
  810.6 10.6 collective-permute-start.1
  821.4 9.7 collective-permute-start.1
  1177.7 16.2 %collective-permute-start.21 = (f32[2,128]{1,0:T(2,128)S(1)}, f32[2,128]{1,0:T(2,128)S(1)}, u32[]{:S(2)}, u32[]{:S(2)}) collective-permute-start(f32[2,128]{1,0:T(2,128)S(1)} %add.282), channel_id=1, source_target_pairs={{0,64},{8,72},{16,80},{24,88},{32,96},{40,104},{48,112},{56,120},{... | collective-permute-start | bytes 3080 | tf_op jit(solution)/shard_map/ppermute | solution.py:196
  1178.5 23.2 %collective-permute-start.14 = (bf16[256,2,128]{0,2,1:T(8,128)(2,1)S(1)}, bf16[256,2,128]{0,2,1:T(8,128)(2,1)S(1)}, u32[]{:S(2)}, u32[]{:S(2)}) collective-permute-start(bf16[256,2,128]{0,2,1:T(8,128)(2,1)S(1)} %get-tuple-element.2469), channel_id=1, source_target_pairs={{8,0},{16,8},{24,16},{32,24},{40,32},{48,40},{56,48},{64,56},{72,6... | collective-permute-start | bytes 393224 | tf_op jit(solution)/shard_map/ppermute | solution.py:15
  1180.4 25.8 %collective-permute-start.15 = (bf16[256,2,128]{0,2,1:T(8,128)(2,1)S(1)}, bf16[256,2,128]{0,2,1:T(8,128)(2,1)S(1)}, u32[]{:S(2)}, u32[]{:S(2)}) collective-permute-start(bf16[256,2,128]{0,2,1:T(8,128)(2,1)S(1)} %get-tuple-element.2472), channel_id=1, source_target_pairs={{16,0},{24,8},{32,16},{40,24},{48,32},{56,40},{64,48},{72,56},{80,... | collective-permute-start | bytes 393224 | tf_op jit(solution)/shard_map/ppermute | solution.py:15
  1182.9 29.2 %collective-permute-start.16 = (bf16[256,2,128]{0,2,1:T(8,128)(2,1)S(1)}, bf16[256,2,128]{0,2,1:T(8,128)(2,1)S(1)}, u32[]{:S(2)}, u32[]{:S(2)}) collective-permute-start(bf16[256,2,128]{0,2,1:T(8,128)(2,1)S(1)} %get-tuple-element.2471), channel_id=1, source_target_pairs={{24,0},{32,8},{40,16},{48,24},{56,32},{64,40},{72,48},{80,56},{88,... | collective-permute-start | bytes 393224 | tf_op jit(solution)/shard_map/ppermute | solution.py:15
  1192.0 22.0 %collective-permute-start.17 = (bf16[256,2,128]{0,2,1:T(8,128)(2,1)S(1)}, bf16[256,2,128]{0,2,1:T(8,128)(2,1)S(1)}, u32[]{:S(2)}, u32[]{:S(2)}) collective-permute-start(bf16[256,2,128]{0,2,1:T(8,128)(2,1)S(1)} %get-tuple-element.2470), channel_id=1, source_target_pairs={{32,0},{40,8},{48,16},{56,24},{64,32},{72,40},{80,48},{88,56},{96,... | collective-permute-start | bytes 393224 | tf_op jit(solution)/shard_map/ppermute | solution.py:15
  1199.1 16.7 %collective-permute-start.10 = (bf16[256,2,128]{2,0,1:T(8,128)(2,1)S(1)}, bf16[256,2,128]{2,0,1:T(8,128)(2,1)S(1)}, u32[]{:S(2)}, u32[]{:S(2)}) collective-permute-start(bf16[256,2,128]{2,0,1:T(8,128)(2,1)S(1)} %get-tuple-element.2473), channel_id=1, source_target_pairs={{8,0},{16,8},{24,16},{32,24},{40,32},{48,40},{56,48},{64,56},{72,6... | collective-permute-start | bytes 393224 | tf_op jit(solution)/shard_map/ppermute | solution.py:15
  1201.7 14.5 %collective-permute-start.11 = (bf16[256,2,128]{2,0,1:T(8,128)(2,1)S(1)}, bf16[256,2,128]{2,0,1:T(8,128)(2,1)S(1)}, u32[]{:S(2)}, u32[]{:S(2)}) collective-permute-start(bf16[256,2,128]{2,0,1:T(8,128)(2,1)S(1)} %get-tuple-element.2476), channel_id=1, source_target_pairs={{16,0},{24,8},{32,16},{40,24},{48,32},{56,40},{64,48},{72,56},{80,... | collective-permute-start | bytes 393224 | tf_op jit(solution)/shard_map/ppermute | solution.py:15
  1206.2 22.4 %collective-permute-start.12 = (bf16[256,2,128]{2,0,1:T(8,128)(2,1)S(1)}, bf16[256,2,128]{2,0,1:T(8,128)(2,1)S(1)}, u32[]{:S(2)}, u32[]{:S(2)}) collective-permute-start(bf16[256,2,128]{2,0,1:T(8,128)(2,1)S(1)} %get-tuple-element.2475), channel_id=1, source_target_pairs={{24,0},{32,8},{40,16},{48,24},{56,32},{64,40},{72,48},{80,56},{88,... | collective-permute-start | bytes 393224 | tf_op jit(solution)/shard_map/ppermute | solution.py:15
  1212.1 16.5 %collective-permute-start.13 = (bf16[256,2,128]{2,0,1:T(8,128)(2,1)S(1)}, bf16[256,2,128]{2,0,1:T(8,128)(2,1)S(1)}, u32[]{:S(2)}, u32[]{:S(2)}) collective-permute-start(bf16[256,2,128]{2,0,1:T(8,128)(2,1)S(1)} %get-tuple-element.2474), channel_id=1, source_target_pairs={{32,0},{40,8},{48,16},{56,24},{64,32},{72,40},{80,48},{88,56},{96,... | collective-permute-start | bytes 393224 | tf_op jit(solution)/shard_map/ppermute | solution.py:15
  (99 other events, 1122.1 us)
